TPU v7x, 256 devices: a whole 4x4x8 slice. The times are simulated.
256 devices in a mesh: row: 16 (over z_lo, y), col: 8 (over x, core), layer: 2 (over z_hi).
Axes of the slice: x: 4, y: 4, z: 8 (z_hi: 2, z_lo: 4; z = z_hi * 4 + z_lo), core: 2. Of those that a mesh axis runs over, the one named last changes fastest.
Arguments:
- density: float32 [2, 8192, 2048], P('layer', 'row', 'col'), may hold values from -6 to 6
- dens_mask: int32 [2, 128, 32], P('layer', 'row', 'col'), may hold values from 0 to 1, as said below
- hamiltonian: float32 [2, 2048, 16384], P('layer', 'row', 'col'), may hold values from -0.375 to 0.375
- ham_mask: int32 [2, 32, 256], P('layer', None, 'col'), may hold values from 0 to 1, as said below
- filter_mask: int32 [128, 256], P('row', 'col'), may hold values from 0 to 1, as said below
Outputs:
- product: float32 [8192, 16384], P('row', ('col', 'layer'))
Inputs may be any that keep to these rules, and one draw needn't show every extreme that they name: `dens_mask`: 1 where a density block is nonzero, else 0. `ham_mask`: 1 where a Hamiltonian block is nonzero, else 0. `filter_mask`: 1 where a result block is kept, else 0.
All inputs are finite; a program needn't handle non-finite values.
Results may differ from a plain program's by a relative error of at most 0.0001.
Values sent between devices are 32-bit elements; how exact they have to be, the bound alone decides.
No kernel may reach another device: no remote copies, remote signals or barrier semaphores. Data moves between devices by JAX's collectives and lax.ppermute only.
A program may use at most 128 MiB of HBM per device.

v0:
```python
import jax
import jax.numpy as jnp
from jax import lax
from jax.sharding import PartitionSpec as P

BLOCK = 64


def expand(block_mask):
    widened = jnp.repeat(block_mask.astype(jnp.float32), BLOCK, axis=-2)
    return jnp.repeat(widened, BLOCK, axis=-1)


def shards(density, dens_mask, hamiltonian, ham_mask, filter_mask):
    dens_vals = density * expand(dens_mask)
    ham_count = hamiltonian.shape[1]
    row_ids = lax.axis_index("row") * ham_count + jnp.arange(ham_count, dtype=jnp.int32)
    block_ids = row_ids // BLOCK
    one_hot = (
        block_ids[:, None] == jnp.arange(ham_mask.shape[1], dtype=jnp.int32)[None, :]
    ).astype(jnp.float32)
    picked = jnp.dot(
        one_hot,
        ham_mask[0].astype(jnp.float32),
        precision=lax.Precision.HIGHEST,
        preferred_element_type=jnp.float32,
    )
    ham_vals = hamiltonian * jnp.repeat(picked, BLOCK, axis=1)[None]
    kept = expand(filter_mask)
    ham_group = lax.all_gather(ham_vals, "row", axis=1, tiled=True)
    ham_part = ham_group[0]
    partial_value = jnp.dot(
        lax.all_gather(dens_vals, "col", axis=2, tiled=True)[0],
        ham_part,
        precision=lax.Precision.HIGHEST,
        preferred_element_type=jnp.float32,
    )
    return lax.psum_scatter(partial_value * kept, "layer", scatter_dimension=1, tiled=True)


def solution(mesh):
    return jax.shard_map(
        shards,
        mesh=mesh,
        in_specs=(
            P("layer", "row", "col"),
            P("layer", "row", "col"),
            P("layer", "row", "col"),
            P("layer", None, "col"),
            P("row", "col"),
        ),
        out_specs=P("row", ("col", "layer")),
        check_vma=False,
    )
```

profile of v0, /device:TPU:1, one launch (start us, length us, event | category | flops | bytes accessed | tf_op | source)
XLA Modules:
  0.0 426.2 jit_solution(16033029685912236478)
XLA Ops:
  6.5 0.0 copy-start.1
  6.5 0.0 copy-start
  6.5 0.0 all-gather.3.cloned.1.call-start
  6.5 1.3 copy.8
  7.8 0.7 convert_bitcast_fusion
  8.5 0.1 broadcast_in_dim.21
  8.6 0.1 broadcast_in_dim.22
  8.7 0.9 bitcast_multiply_fusion.1
  9.5 0.0 all-gather.3.cloned.1.call-update
  9.6 0.0 all-gather.5.cloned.1.call-start
  9.6 1.6 copy.9
  11.2 0.0 copy-done.1
  11.2 0.2 fusion.8
  11.4 1.1 bitcast_multiply_fusion
  12.5 0.0 all-gather.5.cloned.1.call-update
  12.5 0.0 reduce-scatter.2.cloned.1.call-start
  12.6 0.0 copy-done
  12.6 0.1 copy.10
  12.7 0.1 broadcast_in_dim.26
  12.8 0.1 reshape.35
  12.9 2.5 broadcast_in_dim.27
  15.4 5.5 %copy.11 = f32[512,2048]{1,0:T(8,128)} copy(f32[512,2048]{0,1:T(8,128)} %bitcast.24) | data formatting | bytes 8388608 | tf_op jit(solution)/shard_map/reshape | solution.py:11
  20.8 27.6 %all-gather.3.cloned.1.call-done = f32[1,512,2048]{1,2,0:T(8,128)} async-done(((f32[1,512,256]{1,2,0:T(8,128)}), f32[1,512,2048]{1,2,0:T(8,128)}) %all-gather.3.cloned.1.call-update) | async-done | bytes 4194320 | tf_op jit(solution)/shard_map/all_gather | solution.py:33
  48.5 194.2 %all-gather.5.cloned.1.call-done = f32[1,2048,2048]{1,2,0:T(8,128)} async-done(((f32[1,128,2048]{1,2,0:T(8,128)}), f32[1,2048,2048]{1,2,0:T(8,128)}) %all-gather.5.cloned.1.call-update) | async-done | bytes 16777232 | tf_op jit(solution)/shard_map/all_gather | solution.py:30
  242.7 57.7 %fusion.3 = f32[512,2048]{1,0:T(8,128)} fusion(f32[512,2048]{1,0:T(8,128)} %copy.11, f32[1,2048,2048]{1,2,0:T(8,128)} %all-gather.5.cloned.1.call-done, f32[1,512,2048]{1,2,0:T(8,128)} %all-gather.3.cloned.1.call-done), kind=kOutput, calls=%fused_computation.3 | convolution fusion | flops 25770852352 | bytes 29360128 | tf_op jit(solution)/shard_map/dot_general | solution.py:32
  300.3 0.0 reduce-scatter.2.cloned.1.call-update
  300.3 119.4 %reduce-scatter.2.cloned.1.call-done = f32[512,1024]{1,0:T(8,128)} async-done(((f32[512,2048]{1,0:T(8,128)}), f32[512,1024]{1,0:T(8,128)}) %reduce-scatter.2.cloned.1.call-update) | async-done | bytes 2097168 | tf_op jit(solution)/shard_map/reduce_scatter | solution.py:38
  (2 shorter events, 0.0 us)
Async XLA Ops:
  6.5 4.7 %copy-start.1 = (s32[1,32,32]{2,1,0:T(8,128)S(1)}, s32[1,32,32]{2,1,0:T(8,128)}, u32[]{:S(2)}) copy-start(s32[1,32,32]{2,1,0:T(8,128)} %param.8) | copy-start | bytes 12292
  6.5 6.1 %copy-start = (s32[8,32]{1,0:T(8,128)S(1)}, s32[8,32]{1,0:T(8,128)}, u32[]{:S(2)}) copy-start(s32[8,32]{1,0:T(8,128)} %param.9) | copy-start | bytes 3076
  6.5 41.9 %all-gather.3.cloned.1.call-start = ((), (), s32[]{:S(2)}) async-start(), calls=%async_computation.1 | async-start | bytes 4718592 | tf_op jit(solution)/shard_map/all_gather | solution.py:33
  9.6 233.1 %all-gather.5.cloned.1.call-start = ((), (), s32[]{:S(2)}) async-start(), calls=%async_computation.2 | async-start | bytes 17825792 | tf_op jit(solution)/shard_map/all_gather | solution.py:30
  12.5 407.2 %reduce-scatter.2.cloned.1.call-start = ((), (), s32[]{:S(2)}) async-start(), calls=%async_computation.3 | async-start | bytes 6291456 | tf_op jit(solution)/shard_map/reduce_scatter | solution.py:38
Sparse Core Ops, SparseCore 0:
  9.7 38.7 all-gather.2
  50.2 192.4 all-gather.4
  300.5 119.2 reduce-scatter.1
where the time goes:
time: 426 us
  waiting for transfers between devices  341 us (80%)
  matrix products  57.9 us (14%)
  between operations  13.2 us (3%)
  local copies, waits for them, and re-layouts  11.2 us (3%)
    all_gather x1, waiting for transfers between devices, shards(): ham_group = lax.all_gather(ham_vals, 'row', axis=1, tiled=True)  194 us
    reduce_scatter x1, waiting for transfers between devices, shards(): lax.psum_scatter(partial_value * kept, 'layer', scatter_dimension=1, tile...  119 us
    dot_general x1, matrix products, shards(): jnp.dot(lax.all_gather(dens_vals, 'col', axis=2, tiled=True)[0], ham_part...  57.7 us
    all_gather x1, waiting for transfers between devices, shards(): lax.all_gather(dens_vals, 'col', axis=2, tiled=True)[0]  27.6 us
  transfers between devices with their start and end apart: 3, of which 3 were waited for; matrix products, arithmetic and copies ran while one was open for 3% of the time, Pallas kernels for 0%

commit v1 on v0

--- a/solution.py
+++ b/solution.py
@@ -1,9 +1,41 @@
+import functools
 import jax
 import jax.numpy as jnp
 from jax import lax
 from jax.sharding import PartitionSpec as P
 
 BLOCK = 64
+
+
+def settle_tables(load, bus_axis, dim_k):
+    h_now, v1, n_now = (lax.axis_size(bus_axis), lax.axis_index(bus_axis), load.shape[dim_k])
+    ledger = []
+    for idx, kk in enumerate(load.shape):
+        ledger.append(kk * h_now if idx == dim_k else kk)
+    x_next = lax.dynamic_update_slice_in_dim(
+        jnp.zeros(ledger, load.dtype), load, v1 * n_now, axis=dim_k
+    )
+    state_now = raw_out = load
+    for tick in range(1, h_now // 2 + 1):
+        by_place = []
+        for idx in range(h_now):
+            by_place.append((idx, (idx + 1) % h_now))
+        state_now = lax.ppermute(state_now, bus_axis, by_place)
+        x_next = lax.dynamic_update_slice_in_dim(
+            x_next, state_now, (v1 - tick) % h_now * n_now, axis=dim_k
+        )
+        if 2 * tick < h_now:
+            column = []
+            for idx in range(h_now):
+                column.append((idx, (idx - 1) % h_now))
+            raw_out = lax.ppermute(raw_out, bus_axis, column)
+            x_next = lax.dynamic_update_slice_in_dim(
+                x_next, raw_out, (v1 + tick) % h_now * n_now, axis=dim_k
+            )
+    return x_next
+
+
+work_limits = functools.partial(settle_tables, bus_axis="col", dim_k=2)
 
 
 def expand(block_mask):
@@ -30,7 +62,7 @@
     ham_group = lax.all_gather(ham_vals, "row", axis=1, tiled=True)
     ham_part = ham_group[0]
     partial_value = jnp.dot(
-        lax.all_gather(dens_vals, "col", axis=2, tiled=True)[0],
+        work_limits(dens_vals)[0],
         ham_part,
         precision=lax.Precision.HIGHEST,
         preferred_element_type=jnp.float32,

time: 426 us -> 391 us (0.918)
  waiting for transfers between devices: 341 us -> 286 us
  starting transfers between devices: 0.09 us -> 12.7 us
  local copies, waits for them, and re-layouts: 11.2 us -> 18.5 us
    all_gather x1, waiting for transfers between devices: 194 us -> 156 us  [shards(): ham_group = lax.all_gather(ham_vals, 'row', axis=1, tiled=True)]
    all_gather x1 -> x0, waiting for transfers between devices: 27.6 us -> none  [shards(): lax.all_gather(dens_vals, 'col', axis=2, tiled=True)[0]]
    ppermute x0 -> x7, starting transfers between devices: none -> 12.6 us  [the longest x4 7.72 us: settle_tables(): state_now = lax.ppermute(state_now, bus_axis, by_place)]
    ppermute x0 -> x7, waiting for transfers between devices: none -> 10.3 us  [the longest x4 9.55 us: settle_tables(): state_now = lax.ppermute(state_now, bus_axis, by_place)]
    dynamic_update_slice x0 -> x7, local copies, waits for them, and re-layouts: none -> 5.85 us  [the longest x4 3.35 us: settle_tables(): lax.dynamic_update_slice_in_dim(x_next, state_now, (v1 - tick) % h_now *...]
  transfers between devices with their start and end apart: 3 -> 9, of which waited for: 3 -> 7; matrix products, arithmetic and copies ran while one was open for 3% -> 5% of each run, Pallas kernels for 0% -> 0%
where the time goes in v1:
time: 391 us
  waiting for transfers between devices  286 us (73%)
  matrix products  58.5 us (15%)
  local copies, waits for them, and re-layouts  18.5 us (5%)
  between operations  13.5 us (3%)
  starting transfers between devices  12.7 us (3%)
    all_gather x1, waiting for transfers between devices, shards(): ham_group = lax.all_gather(ham_vals, 'row', axis=1, tiled=True)  156 us
    reduce_scatter x1, waiting for transfers between devices, shards(): lax.psum_scatter(partial_value * kept, 'layer', scatter_dimension=1, tile...  119 us
    dot_general x1, matrix products, shards(): jnp.dot(work_limits(dens_vals)[0], ham_part, precision=lax.Precision.HIGH...  57.6 us
    ppermute x4, waiting for transfers between devices, settle_tables(): state_now = lax.ppermute(state_now, bus_axis, by_place)  9.55 us
  transfers between devices with their start and end apart: 9, of which 7 were waited for; matrix products, arithmetic and copies ran while one was open for 5% of the time, Pallas kernels for 0%

profile of v1, /device:TPU:1, one launch (start us, length us, event | category | flops | bytes accessed | tf_op | source)
XLA Modules:
  0.0 390.8 jit_solution(5727720032576247118)
XLA Ops:
  6.5 1.6 copy.9
  8.2 0.9 fusion.5
  9.1 1.1 bitcast_multiply_fusion
  10.3 0.2 copy.8
  10.7 2.5 squeeze.23
  13.2 1.0 bitcast_dynamic-update-slice_fusion.7
  14.1 2.6 collective-permute-start
  16.7 0.6 collective-permute-start.1
  17.3 5.5 %collective-permute-done = f32[1,512,256]{1,2,0:T(8,128)S(1)} collective-permute-done((f32[1,512,256]{1,2,0:T(8,128)S(1)}, f32[1,512,256]{1,2,0:T(8,128)S(1)}, u32[]{:S(2)}, u32[]{:S(2)}) %collective-permute-start) | collective-permute-done | bytes 524320 | tf_op jit(solution)/shard_map/ppermute | solution.py:23
  22.8 2.5 collective-permute-start.2
  25.3 0.3 collective-permute-done.1
  25.6 1.6 collective-permute-start.3
  27.2 0.1 broadcast_in_dim.27
  27.3 0.1 reshape.51
  27.4 2.5 broadcast_in_dim.28
  29.9 5.4 %copy.11 = f32[512,2048]{1,0:T(8,128)} copy(f32[512,2048]{0,1:T(8,128)} %bitcast.36) | data formatting | bytes 8388608 | tf_op jit(solution)/shard_map/reshape | solution.py:43
  35.3 0.2 collective-permute-start.4
  35.5 0.9 bitcast_dynamic-update-slice_fusion.6
  36.4 0.8 bitcast_dynamic-update-slice_fusion.5
  37.2 2.7 collective-permute-start.5
  40.0 0.8 bitcast_dynamic-update-slice_fusion.4
  40.8 0.9 collective-permute-done.4
  41.7 2.5 collective-permute-start.6
  44.1 0.8 bitcast_dynamic-update-slice_fusion.3
  45.0 0.8 bitcast_dynamic-update-slice_fusion.2
  45.8 0.4 collective-permute-done.5
  46.2 0.8 bitcast_dynamic-update-slice_fusion.1
  47.1 3.2 collective-permute-done.6
  50.3 0.8 bitcast_dynamic-update-slice_fusion
  51.1 155.9 %all-gather.2.cloned.1.call-done = f32[1,2048,2048]{1,2,0:T(8,128)} async-done(((f32[1,128,2048]{1,2,0:T(8,128)}), f32[1,2048,2048]{1,2,0:T(8,128)}) %all-gather.2.cloned.1.call-update) | async-done | bytes 16777232 | tf_op jit(solution)/shard_map/all_gather | solution.py:62
  207.0 57.6 %fusion.2 = f32[512,2048]{1,0:T(8,128)} fusion(f32[512,2048]{1,0:T(8,128)} %copy.11, f32[512,2048]{0,1:T(8,128)} %bitcast_dynamic-update-slice_fusion, f32[1,2048,2048]{1,2,0:T(8,128)} %all-gather.2.cloned.1.call-done), kind=kOutput, calls=%fused_computation.2 | convolution fusion | flops 25770852352 | bytes 29360128 | tf_op jit(solution)/shard_map/dot_general | solution.py:64
  264.6 119.4 %reduce-scatter.2.cloned.1.call-done = f32[512,1024]{1,0:T(8,128)} async-done(((f32[512,2048]{1,0:T(8,128)}), f32[512,1024]{1,0:T(8,128)}) %reduce-scatter.2.cloned.1.call-update) | async-done | bytes 2097168 | tf_op jit(solution)/shard_map/reduce_scatter | solution.py:70
  (18 shorter events, 0.3 us)
Async XLA Ops:
  6.5 3.7 copy-start
  6.5 4.0 %copy-start.2 = (s32[1,8,4]{1,2,0:T(4,128)S(1)}, s32[1,8,4]{1,2,0:T(4,128)}, u32[]{:S(2)}) copy-start(s32[1,8,4]{1,2,0:T(4,128)} %param.6) | copy-start | bytes 388
  6.5 200.5 %all-gather.2.cloned.1.call-start = ((), (), s32[]{:S(2)}) async-start(), calls=%async_computation.1 | async-start | bytes 17825792 | tf_op jit(solution)/shard_map/all_gather | solution.py:62
  10.2 16.9 %copy-start.1 = (s32[8,32]{1,0:T(8,128)S(1)}, s32[8,32]{1,0:T(8,128)}, u32[]{:S(2)}) copy-start(s32[8,32]{1,0:T(8,128)} %param.9) | copy-start | bytes 3076
  10.2 373.7 %reduce-scatter.2.cloned.1.call-start = ((), (), s32[]{:S(2)}) async-start(), calls=%async_computation.2 | async-start | bytes 6291456 | tf_op jit(solution)/shard_map/reduce_scatter | solution.py:70
  14.1 8.7 %collective-permute-start = (f32[1,512,256]{1,2,0:T(8,128)S(1)}, f32[1,512,256]{1,2,0:T(8,128)S(1)}, u32[]{:S(2)}, u32[]{:S(2)}) collective-permute-start(f32[1,512,256]{1,2,0:T(8,128)S(1)} %get-tuple-element.6), channel_id=1, source_target_pairs={{0,2},{2,4},{4,6},{6,8},{8,10},{10,12},{12,14},{14,0},{1,3},{3,5},... | collective-permute-start | bytes 1572872 | tf_op jit(solution)/shard_map/ppermute | solution.py:23
  16.7 8.9 %collective-permute-start.1 = (f32[1,512,256]{1,2,0:T(8,128)S(1)}, f32[1,512,256]{1,2,0:T(8,128)S(1)}, u32[]{:S(2)}, u32[]{:S(2)}) collective-permute-start(f32[1,512,256]{1,2,0:T(8,128)S(1)} %get-tuple-element.6), channel_id=1, source_target_pairs={{0,14},{2,0},{4,2},{6,4},{8,6},{10,8},{12,10},{14,12},{1,15},{3,1}... | collective-permute-start | bytes 1572872 | tf_op jit(solution)/shard_map/ppermute | solution.py:31
  22.8 12.5 %collective-permute-start.2 = (f32[1,512,256]{1,2,0:T(8,128)S(1)}, f32[1,512,256]{1,2,0:T(8,128)S(1)}, u32[]{:S(2)}, u32[]{:S(2)}) collective-permute-start(f32[1,512,256]{1,2,0:T(8,128)S(1)} %collective-permute-done), channel_id=1, source_target_pairs={{0,2},{2,4},{4,6},{6,8},{8,10},{10,12},{12,14},{14,0},{1,3},{3,5},... | collective-permute-start | bytes 1572872 | tf_op jit(solution)/shard_map/ppermute | solution.py:23
  25.6 11.6 %collective-permute-start.3 = (f32[1,512,256]{1,2,0:T(8,128)S(1)}, f32[1,512,256]{1,2,0:T(8,128)S(1)}, u32[]{:S(2)}, u32[]{:S(2)}) collective-permute-start(f32[1,512,256]{1,2,0:T(8,128)S(1)} %collective-permute-done.1), channel_id=1, source_target_pairs={{0,14},{2,0},{4,2},{6,4},{8,6},{10,8},{12,10},{14,12},{1,15},{3,1}... | collective-permute-start | bytes 1572872 | tf_op jit(solution)/shard_map/ppermute | solution.py:31
  35.3 6.3 %collective-permute-start.4 = (f32[1,512,256]{1,2,0:T(8,128)S(1)}, f32[1,512,256]{1,2,0:T(8,128)S(1)}, u32[]{:S(2)}, u32[]{:S(2)}) collective-permute-start(f32[1,512,256]{1,2,0:T(8,128)S(1)} %collective-permute-done.2), channel_id=1, source_target_pairs={{0,2},{2,4},{4,6},{6,8},{8,10},{10,12},{12,14},{14,0},{1,3},{3,5},... | collective-permute-start | bytes 1572872 | tf_op jit(solution)/shard_map/ppermute | solution.py:23
  37.2 9.0 %collective-permute-start.5 = (f32[1,512,256]{1,2,0:T(8,128)S(1)}, f32[1,512,256]{1,2,0:T(8,128)S(1)}, u32[]{:S(2)}, u32[]{:S(2)}) collective-permute-start(f32[1,512,256]{1,2,0:T(8,128)S(1)} %collective-permute-done.3), channel_id=1, source_target_pairs={{0,14},{2,0},{4,2},{6,4},{8,6},{10,8},{12,10},{14,12},{1,15},{3,1}... | collective-permute-start | bytes 1572872 | tf_op jit(solution)/shard_map/ppermute | solution.py:31
  41.7 8.6 %collective-permute-start.6 = (f32[1,512,256]{1,2,0:T(8,128)S(1)}, f32[1,512,256]{1,2,0:T(8,128)S(1)}, u32[]{:S(2)}, u32[]{:S(2)}) collective-permute-start(f32[1,512,256]{1,2,0:T(8,128)S(1)} %collective-permute-done.4), channel_id=1, source_target_pairs={{0,2},{2,4},{4,6},{6,8},{8,10},{10,12},{12,14},{14,0},{1,3},{3,5},... | collective-permute-start | bytes 1572872 | tf_op jit(solution)/shard_map/ppermute | solution.py:23
Sparse Core Ops, SparseCore 0:
  10.3 196.6 all-gather.1
  264.7 119.2 reduce-scatter.1
